TPU v7x, 32 devices: a whole 2x2x4 slice. The times are simulated.
32 devices in a mesh: ctx: 16 (over z, x, core), head: 2 (over y).
Axes of the slice: x: 2, y: 2, z: 4, core: 2. Of those that a mesh axis runs over, the one named last changes fastest.
Arguments:
- attn_q: bfloat16 [4096, 8192], P(('ctx', 'head')), may hold values from -8 to 8
- attn_k: bfloat16 [4096, 8192], P(('ctx', 'head')), may hold values from -8 to 8
- attn_v: bfloat16 [4096, 8192], P(('ctx', 'head')), may hold values from -5 to 5
- attn_dout: bfloat16 [4096, 8192], P(('ctx', 'head')), may hold values from -5 to 5
- doc_ids: int32 [4096], replicated, may hold values from 0 to 7, never falling along the last dimension, each value on 1 to 1024 neighbouring positions
Outputs:
- attn_dq: bfloat16 [4096, 8192], P('ctx', 'head')
- attn_dk: bfloat16 [4096, 8192], P('ctx', 'head')
- attn_dv: bfloat16 [4096, 8192], P('ctx', 'head')
Inputs may be any that keep to these rules, and one draw needn't show every extreme that they name: `doc_ids`: document numbers never fall along the window; each document holds 1 to 1024 consecutive tokens, and one holds exactly 1024.
All inputs are finite; a program needn't handle non-finite values.
Results may differ from a plain program's by a relative error of at most 0.0088.
Values may be sent and summed in bfloat16 or wider, within the bound.
No kernel may reach another device: no remote copies, remote signals or barrier semaphores. Data moves between devices by JAX's collectives and lax.ppermute only.
A program may use at most 256 MiB of HBM per device.

v0:
```python
from functools import reduce
import jax
import jax.numpy as jnp
from jax import lax
from jax.sharding import PartitionSpec as P

HEAD_DIM = 128
REACH = 4
masked_value = -1e30


def shifted(value, axis, steps):
    count = lax.axis_size(axis)
    leading, last = (max(0, -steps), min(count, count - steps))
    return lax.ppermute(value, axis, [(source, source + steps) for source in range(leading, last)])


def per_device(attn_q, attn_k, attn_v, attn_dout, doc_ids):
    query, keys, values, dout = (
        lax.all_to_all(attn_q, "head", split_axis=1, concat_axis=0, tiled=True),
        lax.all_to_all(attn_k, "head", split_axis=1, concat_axis=0, tiled=True),
        lax.all_to_all(attn_v, "head", split_axis=1, concat_axis=0, tiled=True),
        lax.all_to_all(attn_dout, "head", split_axis=1, concat_axis=0, tiled=True),
    )
    tok = query.shape[0]
    width = query.shape[1]
    heads_local = width // HEAD_DIM
    ctx_count = lax.axis_size("ctx")
    ctx_pos = lax.axis_index("ctx")
    scale = HEAD_DIM ** (-0.5)

    def head_major(block):
        return jnp.transpose(block.reshape(tok, heads_local, HEAD_DIM), (1, 0, 2))

    q_own = head_major(query)
    k_own = head_major(keys)
    v_own = head_major(values)
    d_own = head_major(dout)
    row_ids = jnp.arange(tok, dtype=jnp.int32)

    def block_info(owner):
        start = jnp.clip(owner * tok, 0, tok * (ctx_count - 1))
        docs = lax.dynamic_slice_in_dim(doc_ids, start, tok)
        return (owner * tok + row_ids, docs, (owner >= 0) & (owner < ctx_count))

    def allowed(q_info, k_info):
        causal = k_info[0][None, :] <= q_info[0][:, None]
        same_doc = k_info[1][None, :] == q_info[1][:, None]
        return causal & same_doc & q_info[2] & k_info[2]

    def scores(q_blk, k_blk, mask):
        raw = jnp.einsum("hqd,hkd->hqk", q_blk, k_blk, preferred_element_type=jnp.float32) * scale
        return jnp.where(mask[None], raw, masked_value)

    own = block_info(ctx_pos)
    key_list = [k_own]
    value_list = [v_own]
    masks = [allowed(own, own)]
    for shift in range(1, REACH + 1):
        far_k, far_v = shifted((k_own, v_own), "ctx", shift)
        key_list.append(far_k)
        value_list.append(far_v)
        masks.append(allowed(own, block_info(ctx_pos - shift)))
    logits = [scores(q_own, key_list[index], masks[index]) for index in range(REACH + 1)]
    top = reduce(jnp.maximum, [jnp.max(item, axis=2) for item in logits])
    denom = reduce(jnp.add, [jnp.sum(jnp.exp(item - top[:, :, None]), axis=2) for item in logits])
    lse = top + jnp.log(denom)
    probs = [
        jnp.where(masks[index][None], jnp.exp(logits[index] - lse[:, :, None]), 0.0)
        for index in range(REACH + 1)
    ]
    attn_out = reduce(
        jnp.add,
        [
            jnp.einsum(
                "hqk,hkd->hqd",
                probs[index].astype(jnp.bfloat16),
                value_list[index],
                preferred_element_type=jnp.float32,
            )
            for index in range(REACH + 1)
        ],
    )
    delta = jnp.sum(d_own.astype(jnp.float32) * attn_out, axis=2)
    shape3 = (heads_local, tok, HEAD_DIM)
    dq_acc = jnp.zeros(shape3, jnp.float32)
    dk_acc = jnp.zeros(shape3, jnp.float32)
    dv_acc = jnp.zeros(shape3, jnp.float32)
    for index in range(REACH + 1):
        k_blk = key_list[index]
        v_blk = value_list[index]
        prob = probs[index]
        prob_bf = prob.astype(jnp.bfloat16)
        dprobs = jnp.einsum("hqd,hkd->hqk", d_own, v_blk, preferred_element_type=jnp.float32)
        dscores = (prob * (dprobs - delta[:, :, None])).astype(jnp.bfloat16)
        dq_acc = dq_acc + jnp.einsum(
            "hqk,hkd->hqd", dscores, k_blk, preferred_element_type=jnp.float32
        )
        if index == 0:
            dk_acc = (
                jnp.einsum("hqk,hqd->hkd", dscores, q_own, preferred_element_type=jnp.float32)
                * scale
            )
            dv_acc = jnp.einsum("hqk,hqd->hkd", prob_bf, d_own, preferred_element_type=jnp.float32)
    for shift in range(1, REACH + 1):
        q_blk, d_blk = shifted((q_own, d_own), "ctx", -shift)
        far_lse, far_delta = shifted((lse, delta), "ctx", -shift)
        mask = allowed(block_info(ctx_pos + shift), own)
        logit = scores(q_blk, k_own, mask)
        prob = jnp.where(mask[None], jnp.exp(logit - far_lse[:, :, None]), 0.0)
        prob_bf = prob.astype(jnp.bfloat16)
        dprobs = jnp.einsum("hqd,hkd->hqk", d_blk, v_own, preferred_element_type=jnp.float32)
        dscores = (prob * (dprobs - far_delta[:, :, None])).astype(jnp.bfloat16)
        dk_acc = (
            dk_acc
            + jnp.einsum("hqk,hqd->hkd", dscores, q_blk, preferred_element_type=jnp.float32) * scale
        )
        dv_acc = dv_acc + jnp.einsum(
            "hqk,hqd->hkd", prob_bf, d_blk, preferred_element_type=jnp.float32
        )

    def token_major(block):
        return jnp.transpose(block, (1, 0, 2)).reshape(tok, width)

    attn_dq = token_major((dq_acc * scale).astype(jnp.bfloat16))
    attn_dk = token_major(dk_acc.astype(jnp.bfloat16))
    attn_dv = token_major(dv_acc.astype(jnp.bfloat16))
    return (attn_dq, attn_dk, attn_dv)


def solution(mesh):
    return jax.shard_map(
        per_device,
        mesh=mesh,
        in_specs=(
            P(("ctx", "head"), None),
            P(("ctx", "head"), None),
            P(("ctx", "head"), None),
            P(("ctx", "head"), None),
            P(),
        ),
        out_specs=(P("ctx", "head"), P("ctx", "head"), P("ctx", "head")),
        check_vma=False,
    )
```

profile of v0, /device:TPU:31, one launch (start us, length us, event | category | flops | bytes accessed | tf_op | source)
XLA Modules:
  0.0 671.9 jit_solution(12698922298471909461)
XLA Ops:
  10.9 20.0 %all-to-all-done.1 = bf16[128,2,4096]{2,0,1:T(8,128)(2,1)S(1)} async-done(((bf16[128,2,4096]{2,0,1:T(8,128)(2,1)}), bf16[128,2,4096]{2,0,1:T(8,128)(2,1)S(1)}, u32[]{:S(2)}, u32[]{:S(2)}) %all-to-all-start.1) | async-done | bytes 2097184 | tf_op jit(solution)/shard_map/all_to_all | solution.py:21
  40.2 19.0 %all-to-all-done = bf16[128,2,4096]{2,0,1:T(8,128)(2,1)S(1)} async-done(((bf16[128,2,4096]{2,0,1:T(8,128)(2,1)}), bf16[128,2,4096]{2,0,1:T(8,128)(2,1)S(1)}, u32[]{:S(2)}, u32[]{:S(2)}) %all-to-all-start) | async-done | bytes 2097184 | tf_op jit(solution)/shard_map/all_to_all | solution.py:20
  72.3 14.2 %all-to-all-done.3 = bf16[128,2,4096]{2,0,1:T(8,128)(2,1)} async-done(((bf16[128,2,4096]{2,0,1:T(8,128)(2,1)}), bf16[128,2,4096]{2,0,1:T(8,128)(2,1)}, u32[]{:S(2)}, u32[]{:S(2)}) %all-to-all-start.3) | async-done | bytes 2097184 | tf_op jit(solution)/shard_map/all_to_all | solution.py:22
  130.9 36.1 %collective-permute-done.3 = bf16[32,256,128]{2,1,0:T(8,128)(2,1)} collective-permute-done((bf16[32,256,128]{2,1,0:T(8,128)(2,1)}, bf16[32,256,128]{2,1,0:T(8,128)(2,1)}, u32[]{:S(2)}, u32[]{:S(2)}) %collective-permute-start.3) | collective-permute-done | bytes 2097184 | tf_op jit(solution)/shard_map/ppermute | solution.py:15
  179.0 82.5 %collective-permute-start.16 = (bf16[32,256,128]{2,1,0:T(8,128)(2,1)}, bf16[32,256,128]{2,1,0:T(8,128)(2,1)}, u32[]{:S(2)}, u32[]{:S(2)}) collective-permute-start(bf16[32,256,128]{2,1,0:T(8,128)(2,1)} %bitcast.136), channel_id=1, source_target_pairs={{6,0},{8,2},{10,4},{12,6},{14,8},{16,10},{18,12},{20,14},{22,16},{... | collective-permute-start | bytes 6291464 | tf_op jit(solution)/shard_map/ppermute | solution.py:15
  261.6 7.2 %fusion.10 = (f32[32,256]{1,0:T(8,128)S(1)}, f32[32,256,256]{1,2,0:T(8,128)}) fusion(pred[256,256]{0,1:T(8,128)(4,1)S(1)} %get-tuple-element.25, bf16[32,256,128]{2,1,0:T(8,128)(2,1)} %collective-permute-done, bf16[256,32,128]{2,1,0:T(8,128)(2,1)S(1)} %bitcast.149), kind=kOutput, calls=%fused_computation.38 | convolution fusion | flops 543154176 | bytes 12681216 | tf_op jit(solution)/shard_map/hqd,hkd->hqk/dot_general | solution.py:52
  268.8 12.7 %exponential_reduce_fusion.3 = (f32[32,256]{1,0:T(8,128)S(1)}, f32[32,256]{1,0:T(8,128)S(1)}, f32[32,256]{1,0:T(8,128)S(1)}, f32[32,256]{1,0:T(8,128)S(1)}, f32[32,256]{1,0:T(8,128)S(1)}) fusion(f32[32,256,256]{1,2,0:T(8,128)} %get-tuple-element.41, f32[32,256]{1,0:T(8,128)S(1)} %maximum_maximum_fusion, pred[256,256]{0,1:T(8,128)(4,1)S(1)} %get-tuple-element.25, ...), kind=kLoop, calls=%fused_computation.21 | loop fusion | flops 41902080 | bytes 42467328 | tf_op jit(solution)/shard_map/reduce_sum | solution.py:66
  284.6 6.2 fusion.24
  290.8 25.0 %collective-permute-start.18 = (bf16[32,256,128]{2,1,0:T(8,128)(2,1)}, bf16[32,256,128]{2,1,0:T(8,128)(2,1)}, u32[]{:S(2)}, u32[]{:S(2)}) collective-permute-start(bf16[32,256,128]{2,1,0:T(8,128)(2,1)} %bitcast.134), channel_id=1, source_target_pairs={{6,0},{8,2},{10,4},{12,6},{14,8},{16,10},{18,12},{20,14},{22,16},{... | collective-permute-start | bytes 6291464 | tf_op jit(solution)/shard_map/ppermute | solution.py:15
  320.4 37.2 %collective-permute-start.14 = (bf16[32,256,128]{2,1,0:T(8,128)(2,1)}, bf16[32,256,128]{2,1,0:T(8,128)(2,1)}, u32[]{:S(2)}, u32[]{:S(2)}) collective-permute-start(bf16[32,256,128]{2,1,0:T(8,128)(2,1)} %bitcast.134), channel_id=1, source_target_pairs={{4,0},{6,2},{8,4},{10,6},{12,8},{14,10},{16,12},{18,14},{20,16},{2... | collective-permute-start | bytes 6291464 | tf_op jit(solution)/shard_map/ppermute | solution.py:15
  357.6 6.2 fusion.28
  363.9 9.1 %fusion.108 = f32[32,256,128]{2,1,0:T(8,128)} fusion(bf16[32,256,128]{2,0,1:T(8,128)(2,1)S(1)} %bitcast.163, f32[32,256,256]{1,2,0:T(8,128)} %get-tuple-element.39, f32[32,256]{1,0:T(8,128)S(1)} %log_add_fusion, pred[256,256]{0,1:T(8,128)(4,1)S(1)} %get-tuple-element.24), kind=kOutput, calls=%fused_computation.128 | convolution fusion | flops 547356672 | bytes 14778368 | tf_op jit(solution)/shard_map/hqk,hkd->hqd/dot_general | solution.py:75
  372.9 17.5 %collective-permute-done.7 = bf16[32,256,128]{2,1,0:T(8,128)(2,1)} collective-permute-done((bf16[32,256,128]{2,1,0:T(8,128)(2,1)}, bf16[32,256,128]{2,1,0:T(8,128)(2,1)}, u32[]{:S(2)}, u32[]{:S(2)}) %collective-permute-start.7) | collective-permute-done | bytes 2097184 | tf_op jit(solution)/shard_map/ppermute | solution.py:15
  393.3 14.4 %multiply_reduce_fusion = f32[32,256]{1,0:T(8,128)S(1)} fusion(f32[32,256,128]{2,1,0:T(8,128)} %fusion.24, f32[32,256,128]{2,1,0:T(8,128)} %fusion.26, f32[32,256,128]{2,1,0:T(8,128)} %fusion.108, f32[32,256,128]{2,1,0:T(8,128)} %fusion.28, bf16[32,256,128]{2,1,0:T(8,128)(2,1)} %collective-permute-done.7, f32[32,256,256]{1,2,0:T(8,128)} %copy-done, ...), kind=kOutput, calls=%fused_computation.57 | convolution fusion | flops 554688512 | bytes 29491200 | tf_op jit(solution)/shard_map/hqk,hkd->hqd/dot_general | solution.py:75
  407.7 10.3 %multiply_convert_fusion.8 = bf16[32,256,256]{1,2,0:T(8,128)(2,1)} fusion(f32[32,256,256]{1,2,0:T(8,128)} %get-tuple-element.39, f32[32,256]{1,0:T(8,128)S(1)} %multiply_reduce_fusion, f32[32,256]{1,0:T(8,128)S(1)} %log_add_fusion, pred[256,256]{0,1:T(8,128)(4,1)S(1)} %get-tuple-element.24, bf16[256,32,128]{2,1,0:T(8,128)(2,1)} %bitcast.162, ...), kind=kOutput, calls=%fused_computation.12 | convolution fusion | flops 551550976 | bytes 16908288 | tf_op jit(solution)/shard_map/hqd,hkd->hqk/dot_general | solution.py:94
  418.0 11.7 %fusion.64 = f32[32,256,128]{1,2,0:T(8,128)} fusion(bf16[32,256,128]{2,1,0:T(8,128)(2,1)} %collective-permute-done.2, f32[32,256,256]{1,2,0:T(8,128)} %copy-done.5, f32[32,256]{1,0:T(8,128)S(1)} %multiply_reduce_fusion, f32[32,256]{1,0:T(8,128)S(1)} %log_add_fusion, pred[256,256]{0,1:T(8,128)(4,1)S(1)} %get-tuple-element.27, ...), kind=kOutput, calls=%fused_computation.88 | convolution fusion | flops 1088421888 | bytes 19005440 | tf_op jit(solution)/shard_map/hqk,hkd->hqd/dot_general | solution.py:96
  429.7 11.5 %fusion.63 = f32[32,256,128]{1,2,0:T(8,128)} fusion(bf16[32,256,128]{2,1,0:T(8,128)(2,1)} %collective-permute-done.1, f32[32,256,256]{1,2,0:T(8,128)} %copy-done.6, f32[32,256]{1,0:T(8,128)S(1)} %multiply_reduce_fusion, f32[32,256]{1,0:T(8,128)S(1)} %log_add_fusion, pred[256,256]{0,1:T(8,128)(4,1)S(1)} %get-tuple-element.26, ...), kind=kOutput, calls=%fused_computation.87 | convolution fusion | flops 1088421888 | bytes 19005440 | tf_op jit(solution)/shard_map/hqk,hkd->hqd/dot_general | solution.py:96
  441.2 11.4 %fusion.62 = f32[32,256,128]{1,2,0:T(8,128)} fusion(bf16[32,256,128]{2,1,0:T(8,128)(2,1)} %collective-permute-done, f32[32,256,256]{1,2,0:T(8,128)} %get-tuple-element.41, f32[32,256]{1,0:T(8,128)S(1)} %multiply_reduce_fusion, f32[32,256]{1,0:T(8,128)S(1)} %log_add_fusion, pred[256,256]{0,1:T(8,128)(4,1)S(1)} %get-tuple-element.25, ...), kind=kOutput, calls=%fused_computation.86 | convolution fusion | flops 1088421888 | bytes 19005440 | tf_op jit(solution)/shard_map/hqk,hkd->hqd/dot_general | solution.py:96
  458.4 14.7 %multiply_convert_fusion.10 = bf16[32,256,128]{1,2,0:T(8,128)(2,1)} fusion(f32[32,256,128]{1,2,0:T(8,128)} %fusion.64, f32[32,256,128]{1,2,0:T(8,128)} %fusion.63, f32[32,256,128]{1,2,0:T(8,128)} %fusion.106, f32[32,256,128]{1,2,0:T(8,128)} %fusion.62, bf16[32,256,128]{2,1,0:T(8,128)(2,1)} %collective-permute-done.3, f32[32,256,256]{1,2,0:T(8,128)} %copy-done, ...), kind=kOutput, calls=%fused_computation.51 | convolution fusion | flops 1094713344 | bytes 33685504 | tf_op jit(solution)/shard_map/hqk,hkd->hqd/dot_general | solution.py:96
  474.9 6.1 fusion.169
  483.6 6.3 fusion.170
  492.7 6.1 fusion.171
  504.2 14.1 %collective-permute-done.20 = bf16[32,256,128]{2,1,0:T(8,128)(2,1)S(1)} collective-permute-done((bf16[32,256,128]{2,1,0:T(8,128)(2,1)}, bf16[32,256,128]{2,1,0:T(8,128)(2,1)S(1)}, u32[]{:S(2)}, u32[]{:S(2)}) %collective-permute-start.20) | collective-permute-done | bytes 2097184 | tf_op jit(solution)/shard_map/ppermute | solution.py:15
  541.6 10.9 %fusion.68 = f32[32,256,128]{1,2,0:T(8,128)} fusion(bf16[32,256,128]{2,1,0:T(8,128)(2,1)} %collective-permute-done.16, f32[32,256,256]{1,2,0:T(8,128)} %fusion.169, f32[32,256]{1,0:T(8,128)S(1)} %collective-permute-done.19, f32[32,256]{1,0:T(8,128)S(1)} %collective-permute-done.17, pred[256,256]{0,1:T(8,128)(4,1)S(1)} %get-tuple-element.31, ...), kind=kOutput, calls=%fused_computation.92 | convolution fusion | flops 1088421888 | bytes 19005440 | tf_op jit(solution)/shard_map/hqk,hqd->hkd/dot_general | solution.py:116
  552.5 10.3 %collective-permute-start.11 = (f32[32,256]{1,0:T(8,128)S(1)}, f32[32,256]{1,0:T(8,128)S(1)}, u32[]{:S(2)}, u32[]{:S(2)}) collective-permute-start(f32[32,256]{1,0:T(8,128)S(1)} %multiply_reduce_fusion), channel_id=1, source_target_pairs={{2,0},{4,2},{6,4},{8,6},{10,8},{12,10},{14,12},{16,14},{18,16},{20... | collective-permute-start | bytes 98312 | tf_op jit(solution)/shard_map/ppermute | solution.py:15
  567.6 25.2 %collective-permute-start.23 = (f32[32,256]{1,0:T(8,128)S(1)}, f32[32,256]{1,0:T(8,128)S(1)}, u32[]{:S(2)}, u32[]{:S(2)}) collective-permute-start(f32[32,256]{1,0:T(8,128)S(1)} %multiply_reduce_fusion), channel_id=1, source_target_pairs={{8,0},{10,2},{12,4},{14,6},{16,8},{18,10},{20,12},{22,14},{24,16},... | collective-permute-start | bytes 98312 | tf_op jit(solution)/shard_map/ppermute | solution.py:15
  592.8 10.9 %fusion.67 = f32[32,256,128]{1,2,0:T(8,128)} fusion(bf16[32,256,128]{2,1,0:T(8,128)(2,1)} %collective-permute-done.12, f32[32,256,256]{1,2,0:T(8,128)} %fusion.170, f32[32,256]{1,0:T(8,128)S(1)} %collective-permute-done.15, f32[32,256]{1,0:T(8,128)S(1)} %collective-permute-done.13, pred[256,256]{0,1:T(8,128)(4,1)S(1)} %get-tuple-element.30, ...), kind=kOutput, calls=%fused_computation.91 | convolution fusion | flops 1088421888 | bytes 19005440 | tf_op jit(solution)/shard_map/hqk,hqd->hkd/dot_general | solution.py:116
  605.9 11.0 %fusion.66 = f32[32,256,128]{1,2,0:T(8,128)} fusion(bf16[32,256,128]{2,1,0:T(8,128)(2,1)} %collective-permute-done.8, f32[32,256,256]{1,2,0:T(8,128)} %fusion.171, f32[32,256]{1,0:T(8,128)S(1)} %collective-permute-done.11, f32[32,256]{1,0:T(8,128)S(1)} %collective-permute-done.9, pred[256,256]{0,1:T(8,128)(4,1)S(1)} %get-tuple-element.29, ...), kind=kOutput, calls=%fused_computation.90 | convolution fusion | flops 1088421888 | bytes 19005440 | tf_op jit(solution)/shard_map/hqk,hqd->hkd/dot_general | solution.py:116
  616.9 13.0 %multiply_convert_fusion.9 = bf16[32,256,128]{1,2,0:T(8,128)(2,1)} fusion(f32[32,256,128]{1,2,0:T(8,128)} %fusion.68, f32[32,256,128]{1,2,0:T(8,128)} %fusion.67, f32[32,256,128]{1,2,0:T(8,128)} %fusion.104, f32[32,256,128]{1,2,0:T(8,128)} %fusion.66, bf16[32,256,128]{2,1,0:T(8,128)(2,1)} %copy-done.12, f32[32,256,256]{1,2,0:T(8,128)} %fusion.172, ...), kind=kOutput, calls=%fused_computation.50 | convolution fusion | flops 1094713344 | bytes 33685504 | tf_op jit(solution)/shard_map/hqk,hqd->hkd/dot_general | solution.py:116
  634.2 8.4 %fusion.16 = f32[32,256,128]{1,2,0:T(8,128)} fusion(bf16[32,256,128]{2,1,0:T(8,128)(2,1)} %collective-permute-done.18, f32[32,256,256]{1,2,0:T(8,128)} %fusion.169, f32[32,256]{1,0:T(8,128)S(1)} %collective-permute-done.17, pred[256,256]{0,1:T(8,128)(4,1)S(1)} %get-tuple-element.31), kind=kOutput, calls=%fused_computation.43 | convolution fusion | flops 547356672 | bytes 14778368 | tf_op jit(solution)/shard_map/hqk,hqd->hkd/dot_general | solution.py:118
  642.7 8.5 %fusion.18 = f32[32,256,128]{1,2,0:T(8,128)} fusion(bf16[32,256,128]{2,1,0:T(8,128)(2,1)} %collective-permute-done.14, f32[32,256,256]{1,2,0:T(8,128)} %fusion.170, f32[32,256]{1,0:T(8,128)S(1)} %collective-permute-done.13, pred[256,256]{0,1:T(8,128)(4,1)S(1)} %get-tuple-element.30), kind=kOutput, calls=%fused_computation.44 | convolution fusion | flops 547356672 | bytes 14778368 | tf_op jit(solution)/shard_map/hqk,hqd->hkd/dot_general | solution.py:118
  657.1 11.5 %add_convert_fusion = bf16[32,256,128]{1,2,0:T(8,128)(2,1)S(1)} fusion(f32[32,256,128]{1,2,0:T(8,128)} %fusion.16, f32[32,256,128]{1,2,0:T(8,128)} %fusion.18, f32[32,256,128]{1,2,0:T(8,128)} %fusion.102, f32[32,256,128]{1,2,0:T(8,128)} %fusion.20, bf16[32,256,128]{2,1,0:T(8,128)(2,1)} %collective-permute-done.22, f32[32,256,256]{1,2,0:T(8,128)} %fusion.172, ...), kind=kOutput, calls=%fused_computation.52 | convolution fusion | flops 552599552 | bytes 29458432 | tf_op jit(solution)/shard_map/hqk,hqd->hkd/dot_general | solution.py:118
  (130 shorter events, 161.1 us)
Async XLA Ops:
  3.8 27.1 %all-to-all-start.1 = ((bf16[128,2,4096]{2,0,1:T(8,128)(2,1)}), bf16[128,2,4096]{2,0,1:T(8,128)(2,1)S(1)}, u32[]{:S(2)}, u32[]{:S(2)}) async-start(bf16[128,2,4096]{2,0,1:T(8,128)(2,1)} %bitcast.178), calls=%async_computation.1 | async-start | bytes 4194304 | tf_op jit(solution)/shard_map/all_to_all | solution.py:21
  32.2 27.0 %all-to-all-start = ((bf16[128,2,4096]{2,0,1:T(8,128)(2,1)}), bf16[128,2,4096]{2,0,1:T(8,128)(2,1)S(1)}, u32[]{:S(2)}, u32[]{:S(2)}) async-start(bf16[128,2,4096]{2,0,1:T(8,128)(2,1)} %bitcast.177), calls=%async_computation | async-start | bytes 4194304 | tf_op jit(solution)/shard_map/all_to_all | solution.py:20
  59.2 27.3 %all-to-all-start.3 = ((bf16[128,2,4096]{2,0,1:T(8,128)(2,1)}), bf16[128,2,4096]{2,0,1:T(8,128)(2,1)}, u32[]{:S(2)}, u32[]{:S(2)}) async-start(bf16[128,2,4096]{2,0,1:T(8,128)(2,1)} %bitcast.176), calls=%async_computation.3 | async-start | bytes 4194304 | tf_op jit(solution)/shard_map/all_to_all | solution.py:22
  69.5 55.9 %collective-permute-start.2 = (bf16[32,256,128]{2,1,0:T(8,128)(2,1)}, bf16[32,256,128]{2,1,0:T(8,128)(2,1)}, u32[]{:S(2)}, u32[]{:S(2)}) collective-permute-start(bf16[32,256,128]{2,1,0:T(8,128)(2,1)} %bitcast.135), channel_id=1, source_target_pairs={{0,6},{2,8},{4,10},{6,12},{8,14},{10,16},{12,18},{14,20},{16,22},{... | collective-permute-start | bytes 6291464 | tf_op jit(solution)/shard_map/ppermute | solution.py:15
  86.5 26.4 %all-to-all-start.2 = ((bf16[128,2,4096]{2,0,1:T(8,128)(2,1)}), bf16[128,2,4096]{2,0,1:T(8,128)(2,1)}, u32[]{:S(2)}, u32[]{:S(2)}) async-start(bf16[128,2,4096]{2,0,1:T(8,128)(2,1)} %bitcast.174), calls=%async_computation.2 | async-start | bytes 4194304 | tf_op jit(solution)/shard_map/all_to_all | solution.py:23
  92.5 74.5 %collective-permute-start.3 = (bf16[32,256,128]{2,1,0:T(8,128)(2,1)}, bf16[32,256,128]{2,1,0:T(8,128)(2,1)}, u32[]{:S(2)}, u32[]{:S(2)}) collective-permute-start(bf16[32,256,128]{2,1,0:T(8,128)(2,1)} %bitcast.135), channel_id=1, source_target_pairs={{0,8},{2,10},{4,12},{6,14},{8,16},{10,18},{12,20},{14,22},{16,24},... | collective-permute-start | bytes 6291464 | tf_op jit(solution)/shard_map/ppermute | solution.py:15
  94.0 78.2 %collective-permute-start.1 = (bf16[32,256,128]{2,1,0:T(8,128)(2,1)}, bf16[32,256,128]{2,1,0:T(8,128)(2,1)}, u32[]{:S(2)}, u32[]{:S(2)}) collective-permute-start(bf16[32,256,128]{2,1,0:T(8,128)(2,1)} %bitcast.135), channel_id=1, source_target_pairs={{0,4},{2,6},{4,8},{6,10},{8,12},{10,14},{12,16},{14,18},{16,20},{1... | collective-permute-start | bytes 6291464 | tf_op jit(solution)/shard_map/ppermute | solution.py:15
  96.7 82.3 %collective-permute-start = (bf16[32,256,128]{2,1,0:T(8,128)(2,1)}, bf16[32,256,128]{2,1,0:T(8,128)(2,1)}, u32[]{:S(2)}, u32[]{:S(2)}) collective-permute-start(bf16[32,256,128]{2,1,0:T(8,128)(2,1)} %bitcast.135), channel_id=1, source_target_pairs={{0,2},{2,4},{4,6},{6,8},{8,10},{10,12},{12,14},{14,16},{16,18},{18... | collective-permute-start | bytes 6291464 | tf_op jit(solution)/shard_map/ppermute | solution.py:15
  107.0 174.5 %collective-permute-start.6 = (bf16[32,256,128]{2,1,0:T(8,128)(2,1)}, bf16[32,256,128]{2,1,0:T(8,128)(2,1)}, u32[]{:S(2)}, u32[]{:S(2)}) collective-permute-start(bf16[32,256,128]{2,1,0:T(8,128)(2,1)} %bitcast.133), channel_id=1, source_target_pairs={{0,6},{2,8},{4,10},{6,12},{8,14},{10,16},{12,18},{14,20},{16,22},{... | collective-permute-start | bytes 6291464 | tf_op jit(solution)/shard_map/ppermute | solution.py:15
  125.5 165.3 %collective-permute-start.5 = (bf16[32,256,128]{2,1,0:T(8,128)(2,1)}, bf16[32,256,128]{2,1,0:T(8,128)(2,1)S(1)}, u32[]{:S(2)}, u32[]{:S(2)}) collective-permute-start(bf16[32,256,128]{2,1,0:T(8,128)(2,1)} %bitcast.133), channel_id=1, source_target_pairs={{0,4},{2,6},{4,8},{6,10},{8,12},{10,14},{12,16},{14,18},{16,20},{1... | collective-permute-start | bytes 6291464 | tf_op jit(solution)/shard_map/ppermute | solution.py:15
  130.9 153.7 %copy-start.5 = (f32[32,256,256]{1,2,0:T(8,128)}, f32[32,256,256]{1,2,0:T(8,128)S(1)}, u32[]{:S(2)}) copy-start(f32[32,256,256]{1,2,0:T(8,128)S(1)} %get-tuple-element.35) | copy-start | bytes 25165828
  167.0 153.5 %collective-permute-start.4 = (bf16[32,256,128]{2,1,0:T(8,128)(2,1)}, bf16[32,256,128]{2,1,0:T(8,128)(2,1)}, u32[]{:S(2)}, u32[]{:S(2)}) collective-permute-start(bf16[32,256,128]{2,1,0:T(8,128)(2,1)} %bitcast.133), channel_id=1, source_target_pairs={{0,2},{2,4},{4,6},{6,8},{8,10},{10,12},{12,14},{14,16},{16,18},{18... | collective-permute-start | bytes 6291464 | tf_op jit(solution)/shard_map/ppermute | solution.py:15
  172.2 96.6 %copy-start = (f32[32,256,256]{1,2,0:T(8,128)}, f32[32,256,256]{1,2,0:T(8,128)S(1)}, u32[]{:S(2)}) copy-start(f32[32,256,256]{1,2,0:T(8,128)S(1)} %get-tuple-element.33) | copy-start | bytes 25165828
  172.2 218.2 %collective-permute-start.7 = (bf16[32,256,128]{2,1,0:T(8,128)(2,1)}, bf16[32,256,128]{2,1,0:T(8,128)(2,1)}, u32[]{:S(2)}, u32[]{:S(2)}) collective-permute-start(bf16[32,256,128]{2,1,0:T(8,128)(2,1)} %bitcast.133), channel_id=1, source_target_pairs={{0,8},{2,10},{4,12},{6,14},{8,16},{10,18},{12,20},{14,22},{16,24},... | collective-permute-start | bytes 6291464 | tf_op jit(solution)/shard_map/ppermute | solution.py:15
  179.0 136.8 %copy-start.6 = (f32[32,256,256]{1,2,0:T(8,128)}, f32[32,256,256]{1,2,0:T(8,128)S(1)}, u32[]{:S(2)}) copy-start(f32[32,256,256]{1,2,0:T(8,128)S(1)} %get-tuple-element.37) | copy-start | bytes 25165828
  179.0 294.1 %collective-permute-start.16 = (bf16[32,256,128]{2,1,0:T(8,128)(2,1)}, bf16[32,256,128]{2,1,0:T(8,128)(2,1)}, u32[]{:S(2)}, u32[]{:S(2)}) collective-permute-start(bf16[32,256,128]{2,1,0:T(8,128)(2,1)} %bitcast.136), channel_id=1, source_target_pairs={{6,0},{8,2},{10,4},{12,6},{14,8},{16,10},{18,12},{20,14},{22,16},{... | collective-permute-start | bytes 6291464 | tf_op jit(solution)/shard_map/ppermute | solution.py:15
  281.5 199.5 %collective-permute-start.12 = (bf16[32,256,128]{2,1,0:T(8,128)(2,1)}, bf16[32,256,128]{2,1,0:T(8,128)(2,1)}, u32[]{:S(2)}, u32[]{:S(2)}) collective-permute-start(bf16[32,256,128]{2,1,0:T(8,128)(2,1)} %bitcast.136), channel_id=1, source_target_pairs={{4,0},{6,2},{8,4},{10,6},{12,8},{14,10},{16,12},{18,14},{20,16},{2... | collective-permute-start | bytes 6291464 | tf_op jit(solution)/shard_map/ppermute | solution.py:15
  290.8 66.8 %slice-start.1 = ((s8[8388608]{0:T(1024)(128)(4,1)}), s8[4194304]{0:T(1024)(128)(4,1)S(1)}, s32[]{:S(2)}) async-start(s8[8388608]{0:T(1024)(128)(4,1)} %bitcast.159), calls=%async_computation.5 | async-start | bytes 8388608
  290.8 241.2 %collective-permute-start.18 = (bf16[32,256,128]{2,1,0:T(8,128)(2,1)}, bf16[32,256,128]{2,1,0:T(8,128)(2,1)}, u32[]{:S(2)}, u32[]{:S(2)}) collective-permute-start(bf16[32,256,128]{2,1,0:T(8,128)(2,1)} %bitcast.134), channel_id=1, source_target_pairs={{6,0},{8,2},{10,4},{12,6},{14,8},{16,10},{18,12},{20,14},{22,16},{... | collective-permute-start | bytes 6291464 | tf_op jit(solution)/shard_map/ppermute | solution.py:15
  320.4 232.1 %collective-permute-start.14 = (bf16[32,256,128]{2,1,0:T(8,128)(2,1)}, bf16[32,256,128]{2,1,0:T(8,128)(2,1)}, u32[]{:S(2)}, u32[]{:S(2)}) collective-permute-start(bf16[32,256,128]{2,1,0:T(8,128)(2,1)} %bitcast.134), channel_id=1, source_target_pairs={{4,0},{6,2},{8,4},{10,6},{12,8},{14,10},{16,12},{18,14},{20,16},{2... | collective-permute-start | bytes 6291464 | tf_op jit(solution)/shard_map/ppermute | solution.py:15
  390.4 99.4 %collective-permute-start.8 = (bf16[32,256,128]{2,1,0:T(8,128)(2,1)}, bf16[32,256,128]{2,1,0:T(8,128)(2,1)}, u32[]{:S(2)}, u32[]{:S(2)}) collective-permute-start(bf16[32,256,128]{2,1,0:T(8,128)(2,1)} %bitcast.136), channel_id=1, source_target_pairs={{2,0},{4,2},{6,4},{8,6},{10,8},{12,10},{14,12},{16,14},{18,16},{20... | collective-permute-start | bytes 6291464 | tf_op jit(solution)/shard_map/ppermute | solution.py:15
  473.1 45.2 %collective-permute-start.20 = (bf16[32,256,128]{2,1,0:T(8,128)(2,1)}, bf16[32,256,128]{2,1,0:T(8,128)(2,1)S(1)}, u32[]{:S(2)}, u32[]{:S(2)}) collective-permute-start(bf16[32,256,128]{2,1,0:T(8,128)(2,1)} %bitcast.136), channel_id=1, source_target_pairs={{8,0},{10,2},{12,4},{14,6},{16,8},{18,10},{20,12},{22,14},{24,16},... | collective-permute-start | bytes 6291464 | tf_op jit(solution)/shard_map/ppermute | solution.py:15
  481.0 122.8 %collective-permute-start.10 = (bf16[32,256,128]{2,1,0:T(8,128)(2,1)}, bf16[32,256,128]{2,1,0:T(8,128)(2,1)}, u32[]{:S(2)}, u32[]{:S(2)}) collective-permute-start(bf16[32,256,128]{2,1,0:T(8,128)(2,1)} %bitcast.134), channel_id=1, source_target_pairs={{2,0},{4,2},{6,4},{8,6},{10,8},{12,10},{14,12},{16,14},{18,16},{20... | collective-permute-start | bytes 6291464 | tf_op jit(solution)/shard_map/ppermute | solution.py:15
  489.8 47.9 %collective-permute-start.19 = (f32[32,256]{1,0:T(8,128)S(1)}, f32[32,256]{1,0:T(8,128)S(1)}, u32[]{:S(2)}, u32[]{:S(2)}) collective-permute-start(f32[32,256]{1,0:T(8,128)S(1)} %multiply_reduce_fusion), channel_id=1, source_target_pairs={{6,0},{8,2},{10,4},{12,6},{14,8},{16,10},{18,12},{20,14},{22,16},{... | collective-permute-start | bytes 98312 | tf_op jit(solution)/shard_map/ppermute | solution.py:15
  518.3 20.9 %collective-permute-start.17 = (f32[32,256]{1,0:T(8,128)S(1)}, f32[32,256]{1,0:T(8,128)S(1)}, u32[]{:S(2)}, u32[]{:S(2)}) collective-permute-start(f32[32,256]{1,0:T(8,128)S(1)} %log_add_fusion), channel_id=1, source_target_pairs={{6,0},{8,2},{10,4},{12,6},{14,8},{16,10},{18,12},{20,14},{22,16},{... | collective-permute-start | bytes 98312 | tf_op jit(solution)/shard_map/ppermute | solution.py:15
  532.1 84.9 %collective-permute-start.22 = (bf16[32,256,128]{2,1,0:T(8,128)(2,1)}, bf16[32,256,128]{2,1,0:T(8,128)(2,1)}, u32[]{:S(2)}, u32[]{:S(2)}) collective-permute-start(bf16[32,256,128]{2,1,0:T(8,128)(2,1)} %bitcast.134), channel_id=1, source_target_pairs={{8,0},{10,2},{12,4},{14,6},{16,8},{18,10},{20,12},{22,14},{24,16},... | collective-permute-start | bytes 6291464 | tf_op jit(solution)/shard_map/ppermute | solution.py:15
  537.8 25.1 %collective-permute-start.15 = (f32[32,256]{1,0:T(8,128)S(1)}, f32[32,256]{1,0:T(8,128)S(1)}, u32[]{:S(2)}, u32[]{:S(2)}) collective-permute-start(f32[32,256]{1,0:T(8,128)S(1)} %multiply_reduce_fusion), channel_id=1, source_target_pairs={{4,0},{6,2},{8,4},{10,6},{12,8},{14,10},{16,12},{18,14},{20,16},{2... | collective-permute-start | bytes 98312 | tf_op jit(solution)/shard_map/ppermute | solution.py:15
  539.2 28.4 %collective-permute-start.13 = (f32[32,256]{1,0:T(8,128)S(1)}, f32[32,256]{1,0:T(8,128)S(1)}, u32[]{:S(2)}, u32[]{:S(2)}) collective-permute-start(f32[32,256]{1,0:T(8,128)S(1)} %log_add_fusion), channel_id=1, source_target_pairs={{4,0},{6,2},{8,4},{10,6},{12,8},{14,10},{16,12},{18,14},{20,16},{2... | collective-permute-start | bytes 98312 | tf_op jit(solution)/shard_map/ppermute | solution.py:15
  552.5 53.4 %collective-permute-start.11 = (f32[32,256]{1,0:T(8,128)S(1)}, f32[32,256]{1,0:T(8,128)S(1)}, u32[]{:S(2)}, u32[]{:S(2)}) collective-permute-start(f32[32,256]{1,0:T(8,128)S(1)} %multiply_reduce_fusion), channel_id=1, source_target_pairs={{2,0},{4,2},{6,4},{8,6},{10,8},{12,10},{14,12},{16,14},{18,16},{20... | collective-permute-start | bytes 98312 | tf_op jit(solution)/shard_map/ppermute | solution.py:15
  562.9 43.0 %collective-permute-start.9 = (f32[32,256]{1,0:T(8,128)S(1)}, f32[32,256]{1,0:T(8,128)S(1)}, u32[]{:S(2)}, u32[]{:S(2)}) collective-permute-start(f32[32,256]{1,0:T(8,128)S(1)} %log_add_fusion), channel_id=1, source_target_pairs={{2,0},{4,2},{6,4},{8,6},{10,8},{12,10},{14,12},{16,14},{18,16},{20... | collective-permute-start | bytes 98312 | tf_op jit(solution)/shard_map/ppermute | solution.py:15
  567.6 49.3 %collective-permute-start.23 = (f32[32,256]{1,0:T(8,128)S(1)}, f32[32,256]{1,0:T(8,128)S(1)}, u32[]{:S(2)}, u32[]{:S(2)}) collective-permute-start(f32[32,256]{1,0:T(8,128)S(1)} %multiply_reduce_fusion), channel_id=1, source_target_pairs={{8,0},{10,2},{12,4},{14,6},{16,8},{18,10},{20,12},{22,14},{24,16},... | collective-permute-start | bytes 98312 | tf_op jit(solution)/shard_map/ppermute | solution.py:15
  603.7 13.2 %collective-permute-start.21 = (f32[32,256]{1,0:T(8,128)S(1)}, f32[32,256]{1,0:T(8,128)S(1)}, u32[]{:S(2)}, u32[]{:S(2)}) collective-permute-start(f32[32,256]{1,0:T(8,128)S(1)} %log_add_fusion), channel_id=1, source_target_pairs={{8,0},{10,2},{12,4},{14,6},{16,8},{18,10},{20,12},{22,14},{24,16},... | collective-permute-start | bytes 98312 | tf_op jit(solution)/shard_map/ppermute | solution.py:15
  (20 other events, 313.0 us)
where the time goes:
time: 681 us; the launch traced here: 672 us
  matrix products  245 us (36%)
  starting transfers between devices  242 us (36%)
  waiting for transfers between devices  126 us (19%)
  local copies, waits for them, and re-layouts  43.5 us (6%)
  other arithmetic  14.4 us (2%)
    ppermute x24, starting transfers between devices, shifted(): lax.ppermute(value, axis, [(source, source + steps) for source in range(l...  221 us
    ppermute x24, waiting for transfers between devices, shifted(): lax.ppermute(value, axis, [(source, source + steps) for source in range(l...  67.7 us
    dot_general x5, matrix products, per_device(): jnp.einsum('hqk,hkd->hqd', dscores, k_blk, preferred_element_type=jnp.flo...  55.1 us
    dot_general x9, matrix products, scores(): jnp.einsum('hqd,hkd->hqk', q_blk, k_blk, preferred_element_type=jnp.float32)  49.5 us
    dot_general x4, matrix products, per_device(): jnp.einsum('hqk,hqd->hkd', dscores, q_blk, preferred_element_type=jnp.flo...  45.8 us
    dot_general x5, matrix products, per_device(): jnp.einsum('hqk,hkd->hqd', probs[index].astype(jnp.bfloat16), value_list[...  40.7 us
    dot_general x4, matrix products, per_device(): jnp.einsum('hqk,hqd->hkd', prob_bf, d_blk, preferred_element_type=jnp.flo...  34.4 us
    unnamed x55, local copies, waits for them, and re-layouts  24 us
  transfers between devices with their start and end apart: 28, of which 7 were waited for; matrix products, arithmetic and copies ran while one was open for 36% of the time, Pallas kernels for 0%

commit v1 on v0

--- a/solution.py
+++ b/solution.py
@@ -7,6 +7,12 @@
 HEAD_DIM = 128
 REACH = 4
 masked_value = -1e30
+
+
+def swap_blocks(value, mesh_axis, split, join):
+    cells = jnp.split(value, lax.axis_size(mesh_axis), axis=split)
+    received = lax.all_to_all(jnp.stack(cells), mesh_axis, 0, 0)
+    return jnp.concatenate(received, axis=join)
 
 
 def shifted(value, axis, steps):
@@ -19,7 +25,7 @@
     query, keys, values, dout = (
         lax.all_to_all(attn_q, "head", split_axis=1, concat_axis=0, tiled=True),
         lax.all_to_all(attn_k, "head", split_axis=1, concat_axis=0, tiled=True),
-        lax.all_to_all(attn_v, "head", split_axis=1, concat_axis=0, tiled=True),
+        swap_blocks(attn_v, "head", 1, 0),
         lax.all_to_all(attn_dout, "head", split_axis=1, concat_axis=0, tiled=True),
     )
     tok = query.shape[0]

time: 681 us -> 681 us (level)
  no operation moved by 1% of the time
where the time goes in v1:
time: 681 us; the launch traced here: 672 us
  matrix products  245 us (36%)
  starting transfers between devices  242 us (36%)
  waiting for transfers between devices  125 us (18%)
  local copies, waits for them, and re-layouts  42.1 us (6%)
  other arithmetic  15.9 us (2%)
    ppermute x24, starting transfers between devices, shifted(): lax.ppermute(value, axis, [(source, source + steps) for source in range(l...  221 us
    ppermute x24, waiting for transfers between devices, shifted(): lax.ppermute(value, axis, [(source, source + steps) for source in range(l...  67.7 us
    dot_general x5, matrix products, per_device(): jnp.einsum('hqk,hkd->hqd', dscores, k_blk, preferred_element_type=jnp.flo...  55 us
    dot_general x9, matrix products, scores(): jnp.einsum('hqd,hkd->hqk', q_blk, k_blk, preferred_element_type=jnp.float32)  49.5 us
    dot_general x4, matrix products, per_device(): jnp.einsum('hqk,hqd->hkd', dscores, q_blk, preferred_element_type=jnp.flo...  45.9 us
    dot_general x5, matrix products, per_device(): jnp.einsum('hqk,hkd->hqd', probs[index].astype(jnp.bfloat16), value_list[...  40.7 us
    dot_general x4, matrix products, per_device(): jnp.einsum('hqk,hqd->hkd', prob_bf, d_blk, preferred_element_type=jnp.flo...  34.4 us
    unnamed x55, local copies, waits for them, and re-layouts  24 us
  transfers between devices with their start and end apart: 28, of which 7 were waited for; matrix products, arithmetic and copies ran while one was open for 36% of the time, Pallas kernels for 0%

profile of v1, /device:TPU:31, one launch (start us, length us, event | category | flops | bytes accessed | tf_op | source)
XLA Modules:
  0.0 672.0 jit_solution(7475605377161647644)
XLA Ops:
  10.9 20.0 %all-to-all-done.1 = bf16[128,2,4096]{2,0,1:T(8,128)(2,1)S(1)} async-done(((bf16[128,2,4096]{2,0,1:T(8,128)(2,1)}), bf16[128,2,4096]{2,0,1:T(8,128)(2,1)S(1)}, u32[]{:S(2)}, u32[]{:S(2)}) %all-to-all-start.1) | async-done | bytes 2097184 | tf_op jit(solution)/shard_map/all_to_all | solution.py:27
  40.2 19.0 %all-to-all-done = bf16[128,2,4096]{2,0,1:T(8,128)(2,1)S(1)} async-done(((bf16[128,2,4096]{2,0,1:T(8,128)(2,1)}), bf16[128,2,4096]{2,0,1:T(8,128)(2,1)S(1)}, u32[]{:S(2)}, u32[]{:S(2)}) %all-to-all-start) | async-done | bytes 2097184 | tf_op jit(solution)/shard_map/all_to_all | solution.py:26
  72.3 14.2 %all-to-all-done.2 = bf16[2,128,4096]{2,1,0:T(8,128)(2,1)} async-done(((bf16[2,128,4096]{2,1,0:T(8,128)(2,1)}), bf16[2,128,4096]{2,1,0:T(8,128)(2,1)}, u32[]{:S(2)}, u32[]{:S(2)}) %all-to-all-start.2) | async-done | bytes 2097184 | tf_op jit(solution)/shard_map/all_to_all | solution.py:14
  130.9 36.0 %collective-permute-done.3 = bf16[32,256,128]{2,1,0:T(8,128)(2,1)} collective-permute-done((bf16[32,256,128]{2,1,0:T(8,128)(2,1)}, bf16[32,256,128]{2,1,0:T(8,128)(2,1)}, u32[]{:S(2)}, u32[]{:S(2)}) %collective-permute-start.3) | collective-permute-done | bytes 2097184 | tf_op jit(solution)/shard_map/ppermute | solution.py:21
  179.0 82.5 %collective-permute-start.16 = (bf16[32,256,128]{2,1,0:T(8,128)(2,1)}, bf16[32,256,128]{2,1,0:T(8,128)(2,1)}, u32[]{:S(2)}, u32[]{:S(2)}) collective-permute-start(bf16[32,256,128]{2,1,0:T(8,128)(2,1)} %bitcast.183), channel_id=1, source_target_pairs={{6,0},{8,2},{10,4},{12,6},{14,8},{16,10},{18,12},{20,14},{22,16},{... | collective-permute-start | bytes 6291464 | tf_op jit(solution)/shard_map/ppermute | solution.py:21
  261.5 7.2 %fusion.19 = (f32[32,256]{1,0:T(8,128)S(1)}, f32[32,256,256]{1,2,0:T(8,128)}) fusion(pred[256,256]{0,1:T(8,128)(4,1)S(1)} %get-tuple-element.27, bf16[32,256,128]{2,1,0:T(8,128)(2,1)} %collective-permute-done, bf16[256,32,128]{2,1,0:T(8,128)(2,1)S(1)} %bitcast.196), kind=kOutput, calls=%fused_computation.47 | convolution fusion | flops 543154176 | bytes 12681216 | tf_op jit(solution)/shard_map/hqd,hkd->hqk/dot_general | solution.py:58
  268.7 12.7 %exponential_reduce_fusion.3 = (f32[32,256]{1,0:T(8,128)S(1)}, f32[32,256]{1,0:T(8,128)S(1)}, f32[32,256]{1,0:T(8,128)S(1)}, f32[32,256]{1,0:T(8,128)S(1)}, f32[32,256]{1,0:T(8,128)S(1)}) fusion(f32[32,256,256]{1,2,0:T(8,128)} %get-tuple-element.43, f32[32,256]{1,0:T(8,128)S(1)} %maximum_maximum_fusion, pred[256,256]{0,1:T(8,128)(4,1)S(1)} %get-tuple-element.27, ...), kind=kLoop, calls=%fused_computation.30 | loop fusion | flops 41902080 | bytes 42467328 | tf_op jit(solution)/shard_map/reduce_sum | solution.py:72
  284.6 6.2 fusion.33
  290.8 25.0 %collective-permute-start.18 = (bf16[32,256,128]{2,1,0:T(8,128)(2,1)}, bf16[32,256,128]{2,1,0:T(8,128)(2,1)}, u32[]{:S(2)}, u32[]{:S(2)}) collective-permute-start(bf16[32,256,128]{2,1,0:T(8,128)(2,1)} %bitcast.180), channel_id=1, source_target_pairs={{6,0},{8,2},{10,4},{12,6},{14,8},{16,10},{18,12},{20,14},{22,16},{... | collective-permute-start | bytes 6291464 | tf_op jit(solution)/shard_map/ppermute | solution.py:21
  320.4 37.2 %collective-permute-start.14 = (bf16[32,256,128]{2,1,0:T(8,128)(2,1)}, bf16[32,256,128]{2,1,0:T(8,128)(2,1)}, u32[]{:S(2)}, u32[]{:S(2)}) collective-permute-start(bf16[32,256,128]{2,1,0:T(8,128)(2,1)} %bitcast.180), channel_id=1, source_target_pairs={{4,0},{6,2},{8,4},{10,6},{12,8},{14,10},{16,12},{18,14},{20,16},{2... | collective-permute-start | bytes 6291464 | tf_op jit(solution)/shard_map/ppermute | solution.py:21
  357.6 6.2 fusion.37
  363.8 9.1 %fusion.125 = f32[32,256,128]{2,1,0:T(8,128)} fusion(bf16[32,256,128]{2,0,1:T(8,128)(2,1)S(1)} %bitcast.210, f32[32,256,256]{1,2,0:T(8,128)} %get-tuple-element.41, f32[32,256]{1,0:T(8,128)S(1)} %log_add_fusion, pred[256,256]{0,1:T(8,128)(4,1)S(1)} %get-tuple-element.26), kind=kOutput, calls=%fused_computation.137 | convolution fusion | flops 547356672 | bytes 14778368 | tf_op jit(solution)/shard_map/hqk,hkd->hqd/dot_general | solution.py:81
  372.9 17.5 %collective-permute-done.7 = bf16[32,256,128]{2,1,0:T(8,128)(2,1)} collective-permute-done((bf16[32,256,128]{2,1,0:T(8,128)(2,1)}, bf16[32,256,128]{2,1,0:T(8,128)(2,1)}, u32[]{:S(2)}, u32[]{:S(2)}) %collective-permute-start.7) | collective-permute-done | bytes 2097184 | tf_op jit(solution)/shard_map/ppermute | solution.py:21
  393.3 14.4 %multiply_reduce_fusion = f32[32,256]{1,0:T(8,128)S(1)} fusion(f32[32,256,128]{2,1,0:T(8,128)} %fusion.33, f32[32,256,128]{2,1,0:T(8,128)} %fusion.35, f32[32,256,128]{2,1,0:T(8,128)} %fusion.125, f32[32,256,128]{2,1,0:T(8,128)} %fusion.37, bf16[32,256,128]{2,1,0:T(8,128)(2,1)} %collective-permute-done.7, f32[32,256,256]{1,2,0:T(8,128)} %copy-done, ...), kind=kOutput, calls=%fused_computation.66 | convolution fusion | flops 554688512 | bytes 29491200 | tf_op jit(solution)/shard_map/hqk,hkd->hqd/dot_general | solution.py:81
  407.8 10.3 %fusion.8 = bf16[32,256,256]{1,2,0:T(8,128)(2,1)} fusion(f32[32,256,256]{1,2,0:T(8,128)} %get-tuple-element.41, f32[32,256]{1,0:T(8,128)S(1)} %multiply_reduce_fusion, f32[32,256]{1,0:T(8,128)S(1)} %log_add_fusion, pred[256,256]{0,1:T(8,128)(4,1)S(1)} %get-tuple-element.26, bf16[256,32,128]{2,1,0:T(8,128)(2,1)} %bitcast.209, bf16[256,32,128]{2,1,0:T(8,128)(2,1)} %bitcast.200), kind=kOutput, calls=%fused_computation.17 | convolution fusion | flops 551550976 | bytes 16908288 | tf_op jit(solution)/shard_map/hqd,hkd->hqk/dot_general | solution.py:100
  418.1 11.7 %fusion.75 = f32[32,256,128]{1,2,0:T(8,128)} fusion(bf16[32,256,128]{2,1,0:T(8,128)(2,1)} %collective-permute-done.2, f32[32,256,256]{1,2,0:T(8,128)} %copy-done.5, f32[32,256]{1,0:T(8,128)S(1)} %multiply_reduce_fusion, f32[32,256]{1,0:T(8,128)S(1)} %log_add_fusion, pred[256,256]{0,1:T(8,128)(4,1)S(1)} %get-tuple-element.29, ...), kind=kOutput, calls=%fused_computation.97 | convolution fusion | flops 1088421888 | bytes 19005440 | tf_op jit(solution)/shard_map/hqk,hkd->hqd/dot_general | solution.py:102
  429.7 11.5 %fusion.73 = f32[32,256,128]{1,2,0:T(8,128)} fusion(bf16[32,256,128]{2,1,0:T(8,128)(2,1)} %collective-permute-done.1, f32[32,256,256]{1,2,0:T(8,128)} %copy-done.6, f32[32,256]{1,0:T(8,128)S(1)} %multiply_reduce_fusion, f32[32,256]{1,0:T(8,128)S(1)} %log_add_fusion, pred[256,256]{0,1:T(8,128)(4,1)S(1)} %get-tuple-element.28, ...), kind=kOutput, calls=%fused_computation.96 | convolution fusion | flops 1088421888 | bytes 19005440 | tf_op jit(solution)/shard_map/hqk,hkd->hqd/dot_general | solution.py:102
  441.2 11.4 %fusion.71 = f32[32,256,128]{1,2,0:T(8,128)} fusion(bf16[32,256,128]{2,1,0:T(8,128)(2,1)} %collective-permute-done, f32[32,256,256]{1,2,0:T(8,128)} %get-tuple-element.43, f32[32,256]{1,0:T(8,128)S(1)} %multiply_reduce_fusion, f32[32,256]{1,0:T(8,128)S(1)} %log_add_fusion, pred[256,256]{0,1:T(8,128)(4,1)S(1)} %get-tuple-element.27, ...), kind=kOutput, calls=%fused_computation.95 | convolution fusion | flops 1088421888 | bytes 19005440 | tf_op jit(solution)/shard_map/hqk,hkd->hqd/dot_general | solution.py:102
  458.4 14.7 %multiply_convert_fusion.1 = bf16[32,256,128]{1,2,0:T(8,128)(2,1)} fusion(f32[32,256,128]{1,2,0:T(8,128)} %fusion.75, f32[32,256,128]{1,2,0:T(8,128)} %fusion.73, f32[32,256,128]{1,2,0:T(8,128)} %fusion.123, f32[32,256,128]{1,2,0:T(8,128)} %fusion.71, bf16[32,256,128]{2,1,0:T(8,128)(2,1)} %collective-permute-done.3, f32[32,256,256]{1,2,0:T(8,128)} %copy-done, ...), kind=kOutput, calls=%fused_computation.60 | convolution fusion | flops 1094713344 | bytes 33685504 | tf_op jit(solution)/shard_map/hqk,hkd->hqd/dot_general | solution.py:102
  474.8 6.1 fusion.190
  483.5 6.3 fusion.191
  492.6 6.1 fusion.192
  504.1 14.1 %collective-permute-done.20 = bf16[32,256,128]{2,1,0:T(8,128)(2,1)S(1)} collective-permute-done((bf16[32,256,128]{2,1,0:T(8,128)(2,1)}, bf16[32,256,128]{2,1,0:T(8,128)(2,1)S(1)}, u32[]{:S(2)}, u32[]{:S(2)}) %collective-permute-start.20) | collective-permute-done | bytes 2097184 | tf_op jit(solution)/shard_map/ppermute | solution.py:21
  541.6 10.9 %fusion.83 = f32[32,256,128]{1,2,0:T(8,128)} fusion(bf16[32,256,128]{2,1,0:T(8,128)(2,1)} %collective-permute-done.16, f32[32,256,256]{1,2,0:T(8,128)} %fusion.190, f32[32,256]{1,0:T(8,128)S(1)} %collective-permute-done.19, f32[32,256]{1,0:T(8,128)S(1)} %collective-permute-done.17, pred[256,256]{0,1:T(8,128)(4,1)S(1)} %get-tuple-element.33, ...), kind=kOutput, calls=%fused_computation.101 | convolution fusion | flops 1088421888 | bytes 19005440 | tf_op jit(solution)/shard_map/hqk,hqd->hkd/dot_general | solution.py:122
  552.5 10.3 %collective-permute-start.11 = (f32[32,256]{1,0:T(8,128)S(1)}, f32[32,256]{1,0:T(8,128)S(1)}, u32[]{:S(2)}, u32[]{:S(2)}) collective-permute-start(f32[32,256]{1,0:T(8,128)S(1)} %multiply_reduce_fusion), channel_id=1, source_target_pairs={{2,0},{4,2},{6,4},{8,6},{10,8},{12,10},{14,12},{16,14},{18,16},{20... | collective-permute-start | bytes 98312 | tf_op jit(solution)/shard_map/ppermute | solution.py:21
  567.6 25.2 %collective-permute-start.23 = (f32[32,256]{1,0:T(8,128)S(1)}, f32[32,256]{1,0:T(8,128)S(1)}, u32[]{:S(2)}, u32[]{:S(2)}) collective-permute-start(f32[32,256]{1,0:T(8,128)S(1)} %multiply_reduce_fusion), channel_id=1, source_target_pairs={{8,0},{10,2},{12,4},{14,6},{16,8},{18,10},{20,12},{22,14},{24,16},... | collective-permute-start | bytes 98312 | tf_op jit(solution)/shard_map/ppermute | solution.py:21
  592.8 10.9 %fusion.81 = f32[32,256,128]{1,2,0:T(8,128)} fusion(bf16[32,256,128]{2,1,0:T(8,128)(2,1)} %collective-permute-done.12, f32[32,256,256]{1,2,0:T(8,128)} %fusion.191, f32[32,256]{1,0:T(8,128)S(1)} %collective-permute-done.15, f32[32,256]{1,0:T(8,128)S(1)} %collective-permute-done.13, pred[256,256]{0,1:T(8,128)(4,1)S(1)} %get-tuple-element.32, ...), kind=kOutput, calls=%fused_computation.100 | convolution fusion | flops 1088421888 | bytes 19005440 | tf_op jit(solution)/shard_map/hqk,hqd->hkd/dot_general | solution.py:122
  605.9 11.0 %fusion.79 = f32[32,256,128]{1,2,0:T(8,128)} fusion(bf16[32,256,128]{2,1,0:T(8,128)(2,1)} %collective-permute-done.8, f32[32,256,256]{1,2,0:T(8,128)} %fusion.192, f32[32,256]{1,0:T(8,128)S(1)} %collective-permute-done.11, f32[32,256]{1,0:T(8,128)S(1)} %collective-permute-done.9, pred[256,256]{0,1:T(8,128)(4,1)S(1)} %get-tuple-element.31, ...), kind=kOutput, calls=%fused_computation.99 | convolution fusion | flops 1088421888 | bytes 19005440 | tf_op jit(solution)/shard_map/hqk,hqd->hkd/dot_general | solution.py:122
  616.9 13.1 %multiply_convert_fusion = bf16[32,256,128]{1,2,0:T(8,128)(2,1)} fusion(f32[32,256,128]{1,2,0:T(8,128)} %fusion.83, f32[32,256,128]{1,2,0:T(8,128)} %fusion.81, f32[32,256,128]{1,2,0:T(8,128)} %fusion.121, f32[32,256,128]{1,2,0:T(8,128)} %fusion.79, bf16[32,256,128]{2,1,0:T(8,128)(2,1)} %copy-done.12, f32[32,256,256]{1,2,0:T(8,128)} %fusion.193, ...), kind=kOutput, calls=%fused_computation.59 | convolution fusion | flops 1094713344 | bytes 33685504 | tf_op jit(solution)/shard_map/hqk,hqd->hkd/dot_general | solution.py:122
  634.3 8.4 %fusion.25 = f32[32,256,128]{1,2,0:T(8,128)} fusion(bf16[32,256,128]{2,1,0:T(8,128)(2,1)} %collective-permute-done.18, f32[32,256,256]{1,2,0:T(8,128)} %fusion.190, f32[32,256]{1,0:T(8,128)S(1)} %collective-permute-done.17, pred[256,256]{0,1:T(8,128)(4,1)S(1)} %get-tuple-element.33), kind=kOutput, calls=%fused_computation.52 | convolution fusion | flops 547356672 | bytes 14778368 | tf_op jit(solution)/shard_map/hqk,hqd->hkd/dot_general | solution.py:124
  642.7 8.5 %fusion.27 = f32[32,256,128]{1,2,0:T(8,128)} fusion(bf16[32,256,128]{2,1,0:T(8,128)(2,1)} %collective-permute-done.14, f32[32,256,256]{1,2,0:T(8,128)} %fusion.191, f32[32,256]{1,0:T(8,128)S(1)} %collective-permute-done.13, pred[256,256]{0,1:T(8,128)(4,1)S(1)} %get-tuple-element.32), kind=kOutput, calls=%fused_computation.53 | convolution fusion | flops 547356672 | bytes 14778368 | tf_op jit(solution)/shard_map/hqk,hqd->hkd/dot_general | solution.py:124
  657.2 11.5 %add_convert_fusion = bf16[32,256,128]{1,2,0:T(8,128)(2,1)S(1)} fusion(f32[32,256,128]{1,2,0:T(8,128)} %fusion.25, f32[32,256,128]{1,2,0:T(8,128)} %fusion.27, f32[32,256,128]{1,2,0:T(8,128)} %fusion.119, f32[32,256,128]{1,2,0:T(8,128)} %fusion.29, bf16[32,256,128]{2,1,0:T(8,128)(2,1)} %collective-permute-done.22, f32[32,256,256]{1,2,0:T(8,128)} %fusion.193, ...), kind=kOutput, calls=%fused_computation.61 | convolution fusion | flops 552599552 | bytes 29458432 | tf_op jit(solution)/shard_map/hqk,hqd->hkd/dot_general | solution.py:124
  (131 shorter events, 161.1 us)
Async XLA Ops:
  3.8 27.1 %all-to-all-start.1 = ((bf16[128,2,4096]{2,0,1:T(8,128)(2,1)}), bf16[128,2,4096]{2,0,1:T(8,128)(2,1)S(1)}, u32[]{:S(2)}, u32[]{:S(2)}) async-start(bf16[128,2,4096]{2,0,1:T(8,128)(2,1)} %bitcast.224), calls=%async_computation.1 | async-start | bytes 4194304 | tf_op jit(solution)/shard_map/all_to_all | solution.py:27
  32.2 27.0 %all-to-all-start = ((bf16[128,2,4096]{2,0,1:T(8,128)(2,1)}), bf16[128,2,4096]{2,0,1:T(8,128)(2,1)S(1)}, u32[]{:S(2)}, u32[]{:S(2)}) async-start(bf16[128,2,4096]{2,0,1:T(8,128)(2,1)} %bitcast.223), calls=%async_computation | async-start | bytes 4194304 | tf_op jit(solution)/shard_map/all_to_all | solution.py:26
  59.2 27.3 %all-to-all-start.2 = ((bf16[2,128,4096]{2,1,0:T(8,128)(2,1)}), bf16[2,128,4096]{2,1,0:T(8,128)(2,1)}, u32[]{:S(2)}, u32[]{:S(2)}) async-start(bf16[2,128,4096]{2,1,0:T(8,128)(2,1)} %pad_maximum_fusion), calls=%async_computation.2 | async-start | bytes 4194304 | tf_op jit(solution)/shard_map/all_to_all | solution.py:14
  69.5 55.9 %collective-permute-start.2 = (bf16[32,256,128]{2,1,0:T(8,128)(2,1)}, bf16[32,256,128]{2,1,0:T(8,128)(2,1)}, u32[]{:S(2)}, u32[]{:S(2)}) collective-permute-start(bf16[32,256,128]{2,1,0:T(8,128)(2,1)} %bitcast.182), channel_id=1, source_target_pairs={{0,6},{2,8},{4,10},{6,12},{8,14},{10,16},{12,18},{14,20},{16,22},{... | collective-permute-start | bytes 6291464 | tf_op jit(solution)/shard_map/ppermute | solution.py:21
  86.5 26.4 %all-to-all-start.3 = ((bf16[128,2,4096]{2,0,1:T(8,128)(2,1)}), bf16[128,2,4096]{2,0,1:T(8,128)(2,1)}, u32[]{:S(2)}, u32[]{:S(2)}) async-start(bf16[128,2,4096]{2,0,1:T(8,128)(2,1)} %bitcast.221), calls=%async_computation.3 | async-start | bytes 4194304 | tf_op jit(solution)/shard_map/all_to_all | solution.py:29
  92.5 74.5 %collective-permute-start.3 = (bf16[32,256,128]{2,1,0:T(8,128)(2,1)}, bf16[32,256,128]{2,1,0:T(8,128)(2,1)}, u32[]{:S(2)}, u32[]{:S(2)}) collective-permute-start(bf16[32,256,128]{2,1,0:T(8,128)(2,1)} %bitcast.182), channel_id=1, source_target_pairs={{0,8},{2,10},{4,12},{6,14},{8,16},{10,18},{12,20},{14,22},{16,24},... | collective-permute-start | bytes 6291464 | tf_op jit(solution)/shard_map/ppermute | solution.py:21
  94.0 78.2 %collective-permute-start.1 = (bf16[32,256,128]{2,1,0:T(8,128)(2,1)}, bf16[32,256,128]{2,1,0:T(8,128)(2,1)}, u32[]{:S(2)}, u32[]{:S(2)}) collective-permute-start(bf16[32,256,128]{2,1,0:T(8,128)(2,1)} %bitcast.182), channel_id=1, source_target_pairs={{0,4},{2,6},{4,8},{6,10},{8,12},{10,14},{12,16},{14,18},{16,20},{1... | collective-permute-start | bytes 6291464 | tf_op jit(solution)/shard_map/ppermute | solution.py:21
  96.7 82.3 %collective-permute-start = (bf16[32,256,128]{2,1,0:T(8,128)(2,1)}, bf16[32,256,128]{2,1,0:T(8,128)(2,1)}, u32[]{:S(2)}, u32[]{:S(2)}) collective-permute-start(bf16[32,256,128]{2,1,0:T(8,128)(2,1)} %bitcast.182), channel_id=1, source_target_pairs={{0,2},{2,4},{4,6},{6,8},{8,10},{10,12},{12,14},{14,16},{16,18},{18... | collective-permute-start | bytes 6291464 | tf_op jit(solution)/shard_map/ppermute | solution.py:21
  107.0 174.5 %collective-permute-start.6 = (bf16[32,256,128]{2,1,0:T(8,128)(2,1)}, bf16[32,256,128]{2,1,0:T(8,128)(2,1)}, u32[]{:S(2)}, u32[]{:S(2)}) collective-permute-start(bf16[32,256,128]{2,1,0:T(8,128)(2,1)} %bitcast.181), channel_id=1, source_target_pairs={{0,6},{2,8},{4,10},{6,12},{8,14},{10,16},{12,18},{14,20},{16,22},{... | collective-permute-start | bytes 6291464 | tf_op jit(solution)/shard_map/ppermute | solution.py:21
  125.5 165.3 %collective-permute-start.5 = (bf16[32,256,128]{2,1,0:T(8,128)(2,1)}, bf16[32,256,128]{2,1,0:T(8,128)(2,1)S(1)}, u32[]{:S(2)}, u32[]{:S(2)}) collective-permute-start(bf16[32,256,128]{2,1,0:T(8,128)(2,1)} %bitcast.181), channel_id=1, source_target_pairs={{0,4},{2,6},{4,8},{6,10},{8,12},{10,14},{12,16},{14,18},{16,20},{1... | collective-permute-start | bytes 6291464 | tf_op jit(solution)/shard_map/ppermute | solution.py:21
  130.9 153.6 %copy-start.5 = (f32[32,256,256]{1,2,0:T(8,128)}, f32[32,256,256]{1,2,0:T(8,128)S(1)}, u32[]{:S(2)}) copy-start(f32[32,256,256]{1,2,0:T(8,128)S(1)} %get-tuple-element.37) | copy-start | bytes 25165828
  167.0 153.5 %collective-permute-start.4 = (bf16[32,256,128]{2,1,0:T(8,128)(2,1)}, bf16[32,256,128]{2,1,0:T(8,128)(2,1)}, u32[]{:S(2)}, u32[]{:S(2)}) collective-permute-start(bf16[32,256,128]{2,1,0:T(8,128)(2,1)} %bitcast.181), channel_id=1, source_target_pairs={{0,2},{2,4},{4,6},{6,8},{8,10},{10,12},{12,14},{14,16},{16,18},{18... | collective-permute-start | bytes 6291464 | tf_op jit(solution)/shard_map/ppermute | solution.py:21
  172.2 96.6 %copy-start = (f32[32,256,256]{1,2,0:T(8,128)}, f32[32,256,256]{1,2,0:T(8,128)S(1)}, u32[]{:S(2)}) copy-start(f32[32,256,256]{1,2,0:T(8,128)S(1)} %get-tuple-element.35) | copy-start | bytes 25165828
  172.2 218.2 %collective-permute-start.7 = (bf16[32,256,128]{2,1,0:T(8,128)(2,1)}, bf16[32,256,128]{2,1,0:T(8,128)(2,1)}, u32[]{:S(2)}, u32[]{:S(2)}) collective-permute-start(bf16[32,256,128]{2,1,0:T(8,128)(2,1)} %bitcast.181), channel_id=1, source_target_pairs={{0,8},{2,10},{4,12},{6,14},{8,16},{10,18},{12,20},{14,22},{16,24},... | collective-permute-start | bytes 6291464 | tf_op jit(solution)/shard_map/ppermute | solution.py:21
  179.0 136.8 %copy-start.6 = (f32[32,256,256]{1,2,0:T(8,128)}, f32[32,256,256]{1,2,0:T(8,128)S(1)}, u32[]{:S(2)}) copy-start(f32[32,256,256]{1,2,0:T(8,128)S(1)} %get-tuple-element.39) | copy-start | bytes 25165828
  179.0 294.1 %collective-permute-start.16 = (bf16[32,256,128]{2,1,0:T(8,128)(2,1)}, bf16[32,256,128]{2,1,0:T(8,128)(2,1)}, u32[]{:S(2)}, u32[]{:S(2)}) collective-permute-start(bf16[32,256,128]{2,1,0:T(8,128)(2,1)} %bitcast.183), channel_id=1, source_target_pairs={{6,0},{8,2},{10,4},{12,6},{14,8},{16,10},{18,12},{20,14},{22,16},{... | collective-permute-start | bytes 6291464 | tf_op jit(solution)/shard_map/ppermute | solution.py:21
  281.5 199.5 %collective-permute-start.12 = (bf16[32,256,128]{2,1,0:T(8,128)(2,1)}, bf16[32,256,128]{2,1,0:T(8,128)(2,1)}, u32[]{:S(2)}, u32[]{:S(2)}) collective-permute-start(bf16[32,256,128]{2,1,0:T(8,128)(2,1)} %bitcast.183), channel_id=1, source_target_pairs={{4,0},{6,2},{8,4},{10,6},{12,8},{14,10},{16,12},{18,14},{20,16},{2... | collective-permute-start | bytes 6291464 | tf_op jit(solution)/shard_map/ppermute | solution.py:21
  290.8 66.8 %slice-start.1 = ((s8[8388608]{0:T(1024)(128)(4,1)}), s8[4194304]{0:T(1024)(128)(4,1)S(1)}, s32[]{:S(2)}) async-start(s8[8388608]{0:T(1024)(128)(4,1)} %bitcast.206), calls=%async_computation.5 | async-start | bytes 8388608
  290.8 241.2 %collective-permute-start.18 = (bf16[32,256,128]{2,1,0:T(8,128)(2,1)}, bf16[32,256,128]{2,1,0:T(8,128)(2,1)}, u32[]{:S(2)}, u32[]{:S(2)}) collective-permute-start(bf16[32,256,128]{2,1,0:T(8,128)(2,1)} %bitcast.180), channel_id=1, source_target_pairs={{6,0},{8,2},{10,4},{12,6},{14,8},{16,10},{18,12},{20,14},{22,16},{... | collective-permute-start | bytes 6291464 | tf_op jit(solution)/shard_map/ppermute | solution.py:21
  320.4 232.1 %collective-permute-start.14 = (bf16[32,256,128]{2,1,0:T(8,128)(2,1)}, bf16[32,256,128]{2,1,0:T(8,128)(2,1)}, u32[]{:S(2)}, u32[]{:S(2)}) collective-permute-start(bf16[32,256,128]{2,1,0:T(8,128)(2,1)} %bitcast.180), channel_id=1, source_target_pairs={{4,0},{6,2},{8,4},{10,6},{12,8},{14,10},{16,12},{18,14},{20,16},{2... | collective-permute-start | bytes 6291464 | tf_op jit(solution)/shard_map/ppermute | solution.py:21
  390.4 99.4 %collective-permute-start.8 = (bf16[32,256,128]{2,1,0:T(8,128)(2,1)}, bf16[32,256,128]{2,1,0:T(8,128)(2,1)}, u32[]{:S(2)}, u32[]{:S(2)}) collective-permute-start(bf16[32,256,128]{2,1,0:T(8,128)(2,1)} %bitcast.183), channel_id=1, source_target_pairs={{2,0},{4,2},{6,4},{8,6},{10,8},{12,10},{14,12},{16,14},{18,16},{20... | collective-permute-start | bytes 6291464 | tf_op jit(solution)/shard_map/ppermute | solution.py:21
  473.1 45.2 %collective-permute-start.20 = (bf16[32,256,128]{2,1,0:T(8,128)(2,1)}, bf16[32,256,128]{2,1,0:T(8,128)(2,1)S(1)}, u32[]{:S(2)}, u32[]{:S(2)}) collective-permute-start(bf16[32,256,128]{2,1,0:T(8,128)(2,1)} %bitcast.183), channel_id=1, source_target_pairs={{8,0},{10,2},{12,4},{14,6},{16,8},{18,10},{20,12},{22,14},{24,16},... | collective-permute-start | bytes 6291464 | tf_op jit(solution)/shard_map/ppermute | solution.py:21
  480.9 122.8 %collective-permute-start.10 = (bf16[32,256,128]{2,1,0:T(8,128)(2,1)}, bf16[32,256,128]{2,1,0:T(8,128)(2,1)}, u32[]{:S(2)}, u32[]{:S(2)}) collective-permute-start(bf16[32,256,128]{2,1,0:T(8,128)(2,1)} %bitcast.180), channel_id=1, source_target_pairs={{2,0},{4,2},{6,4},{8,6},{10,8},{12,10},{14,12},{16,14},{18,16},{20... | collective-permute-start | bytes 6291464 | tf_op jit(solution)/shard_map/ppermute | solution.py:21
  489.8 47.9 %collective-permute-start.19 = (f32[32,256]{1,0:T(8,128)S(1)}, f32[32,256]{1,0:T(8,128)S(1)}, u32[]{:S(2)}, u32[]{:S(2)}) collective-permute-start(f32[32,256]{1,0:T(8,128)S(1)} %multiply_reduce_fusion), channel_id=1, source_target_pairs={{6,0},{8,2},{10,4},{12,6},{14,8},{16,10},{18,12},{20,14},{22,16},{... | collective-permute-start | bytes 98312 | tf_op jit(solution)/shard_map/ppermute | solution.py:21
  518.3 20.9 %collective-permute-start.17 = (f32[32,256]{1,0:T(8,128)S(1)}, f32[32,256]{1,0:T(8,128)S(1)}, u32[]{:S(2)}, u32[]{:S(2)}) collective-permute-start(f32[32,256]{1,0:T(8,128)S(1)} %log_add_fusion), channel_id=1, source_target_pairs={{6,0},{8,2},{10,4},{12,6},{14,8},{16,10},{18,12},{20,14},{22,16},{... | collective-permute-start | bytes 98312 | tf_op jit(solution)/shard_map/ppermute | solution.py:21
  532.0 84.9 %collective-permute-start.22 = (bf16[32,256,128]{2,1,0:T(8,128)(2,1)}, bf16[32,256,128]{2,1,0:T(8,128)(2,1)}, u32[]{:S(2)}, u32[]{:S(2)}) collective-permute-start(bf16[32,256,128]{2,1,0:T(8,128)(2,1)} %bitcast.180), channel_id=1, source_target_pairs={{8,0},{10,2},{12,4},{14,6},{16,8},{18,10},{20,12},{22,14},{24,16},... | collective-permute-start | bytes 6291464 | tf_op jit(solution)/shard_map/ppermute | solution.py:21
  537.7 25.1 %collective-permute-start.15 = (f32[32,256]{1,0:T(8,128)S(1)}, f32[32,256]{1,0:T(8,128)S(1)}, u32[]{:S(2)}, u32[]{:S(2)}) collective-permute-start(f32[32,256]{1,0:T(8,128)S(1)} %multiply_reduce_fusion), channel_id=1, source_target_pairs={{4,0},{6,2},{8,4},{10,6},{12,8},{14,10},{16,12},{18,14},{20,16},{2... | collective-permute-start | bytes 98312 | tf_op jit(solution)/shard_map/ppermute | solution.py:21
  539.2 28.3 %collective-permute-start.13 = (f32[32,256]{1,0:T(8,128)S(1)}, f32[32,256]{1,0:T(8,128)S(1)}, u32[]{:S(2)}, u32[]{:S(2)}) collective-permute-start(f32[32,256]{1,0:T(8,128)S(1)} %log_add_fusion), channel_id=1, source_target_pairs={{4,0},{6,2},{8,4},{10,6},{12,8},{14,10},{16,12},{18,14},{20,16},{2... | collective-permute-start | bytes 98312 | tf_op jit(solution)/shard_map/ppermute | solution.py:21
  552.5 53.4 %collective-permute-start.11 = (f32[32,256]{1,0:T(8,128)S(1)}, f32[32,256]{1,0:T(8,128)S(1)}, u32[]{:S(2)}, u32[]{:S(2)}) collective-permute-start(f32[32,256]{1,0:T(8,128)S(1)} %multiply_reduce_fusion), channel_id=1, source_target_pairs={{2,0},{4,2},{6,4},{8,6},{10,8},{12,10},{14,12},{16,14},{18,16},{20... | collective-permute-start | bytes 98312 | tf_op jit(solution)/shard_map/ppermute | solution.py:21
  562.8 43.0 %collective-permute-start.9 = (f32[32,256]{1,0:T(8,128)S(1)}, f32[32,256]{1,0:T(8,128)S(1)}, u32[]{:S(2)}, u32[]{:S(2)}) collective-permute-start(f32[32,256]{1,0:T(8,128)S(1)} %log_add_fusion), channel_id=1, source_target_pairs={{2,0},{4,2},{6,4},{8,6},{10,8},{12,10},{14,12},{16,14},{18,16},{20... | collective-permute-start | bytes 98312 | tf_op jit(solution)/shard_map/ppermute | solution.py:21
  567.6 49.3 %collective-permute-start.23 = (f32[32,256]{1,0:T(8,128)S(1)}, f32[32,256]{1,0:T(8,128)S(1)}, u32[]{:S(2)}, u32[]{:S(2)}) collective-permute-start(f32[32,256]{1,0:T(8,128)S(1)} %multiply_reduce_fusion), channel_id=1, source_target_pairs={{8,0},{10,2},{12,4},{14,6},{16,8},{18,10},{20,12},{22,14},{24,16},... | collective-permute-start | bytes 98312 | tf_op jit(solution)/shard_map/ppermute | solution.py:21
  603.7 13.2 %collective-permute-start.21 = (f32[32,256]{1,0:T(8,128)S(1)}, f32[32,256]{1,0:T(8,128)S(1)}, u32[]{:S(2)}, u32[]{:S(2)}) collective-permute-start(f32[32,256]{1,0:T(8,128)S(1)} %log_add_fusion), channel_id=1, source_target_pairs={{8,0},{10,2},{12,4},{14,6},{16,8},{18,10},{20,12},{22,14},{24,16},... | collective-permute-start | bytes 98312 | tf_op jit(solution)/shard_map/ppermute | solution.py:21
  (20 other events, 313.1 us)
